TPU v7x, 512 devices: a whole 4x8x8 slice. The times are simulated.
512 devices in a mesh: seq: 32 (over x_lo, z, core), tensor: 16 (over x_hi, y).
Axes of the slice: x: 4 (x_hi: 2, x_lo: 2; x = x_hi * 2 + x_lo), y: 8, z: 8, core: 2. Of those that a mesh axis runs over, the one named last changes fastest.
Arguments:
- qkv: bfloat16 [3, 8192, 8192], P(None, 'seq', 'tensor'), may hold values from -6 to 6
- conv_weight: float32 [3, 3, 8192], P(None, None, 'tensor'), may hold values from -3.6 to 3.6
- decay_rate: float32 [16, 8192], P(None, 'tensor'), may hold values from 1e-05 to 0.06
- residue: float32 [16, 8192], P(None, 'tensor'), may hold values from -3 to 3
- skip_gain: float32 [8192], P('tensor'), may hold values from -5 to 5
- out_weight: bfloat16 [8192, 8192], P('seq', 'tensor'), may hold values from -0.125 to 0.125
Outputs:
- mixer_out: bfloat16 [8192, 8192], P('seq', 'tensor')
All inputs are finite; a program needn't handle non-finite values.
Results may differ from a plain program's by a relative error of at most 0.0049.
Values may be sent and summed in bfloat16 or wider, within the bound.
No kernel may reach another device: no remote copies, remote signals or barrier semaphores. Data moves between devices by JAX's collectives and lax.ppermute only.
A program may use at most 64 MiB of HBM per device.

v0:
```python
from functools import partial
import jax
import jax.numpy as jnp
from jax import lax
from jax.sharding import PartitionSpec as P

KS = 3
PRECISE = lax.Precision.HIGHEST


def passed_along(block, axis, distance):
    devices = range(lax.axis_size(axis))
    route = [(i - distance, i) for i in devices if i - distance in devices]
    return lax.ppermute(block, axis, route)


def prefix_2(part, axis, combine, identity):
    place = lax.axis_index(axis)
    gathered = jax.tree.map(lambda a: lax.all_gather(a, axis), part)
    state = jax.tree.map(lambda a, e: jnp.zeros_like(a) + jnp.asarray(e, a.dtype), part, identity)

    def one(step, state):
        return combine(
            state, jax.tree.map(lambda a: lax.dynamic_index_in_dim(a, step, 0, False), gathered)
        )

    return lax.fori_loop(0, place, one, state)


def mode_tables(rate_block, residue_block, length):
    lag_values = jnp.arange(length, dtype=jnp.float32)
    decay_table = jnp.exp(-rate_block[:, None, :] * lag_values[None, :, None])
    mode_weight = residue_block * jnp.sqrt(-jnp.expm1(-2.0 * rate_block))
    return (decay_table, mode_weight)


def toeplitz(filter_taps):
    length = filter_taps.shape[0]
    lag_index = jnp.arange(length)[:, None] - jnp.arange(length)[None, :]
    picked = filter_taps[jnp.maximum(lag_index, 0), :]
    return jnp.where(lag_index[:, :, None] >= 0, picked, 0.0)


def inner_block(block_len, inputs):
    x_block, rate_block, residue_block = inputs
    decay_table, mode_weight = mode_tables(rate_block, residue_block, block_len)
    filter_taps = jnp.einsum("mc,mdc->dc", mode_weight, decay_table, precision=PRECISE)
    inner_part = jnp.einsum("tsc,nsc->ntc", toeplitz(filter_taps), x_block, precision=PRECISE)
    local_state = jnp.einsum("msc,nsc->nmc", decay_table[:, ::-1, :], x_block, precision=PRECISE)
    block_decay = jnp.exp(-rate_block * block_len)

    def advance(state, segment):
        return (state * block_decay + segment, state)

    section_state, entering = lax.scan(
        advance, jnp.zeros(rate_block.shape, jnp.float32), local_state
    )
    return (inner_part, entering, section_state)


def carry_block(block_len, inputs):
    rate_block, residue_block, block_entering, section_entering = inputs
    decay_table, mode_weight = mode_tables(rate_block, residue_block, block_len)
    block_ids = jnp.arange(block_entering.shape[0], dtype=jnp.float32)
    reach_back = jnp.exp(-rate_block[None] * (block_len * block_ids)[:, None, None])
    entering_all = block_entering + reach_back * section_entering[None]
    later_table = decay_table * jnp.exp(-rate_block)[:, None, :]
    return jnp.einsum("mc,mdc,nmc->ndc", mode_weight, later_table, entering_all, precision=PRECISE)


def combine_modes(earlier, later):
    return (earlier[0] * later[0], earlier[1] * later[0] + later[1])


def local(qkv, conv_weight, decay_rate, residue, skip_gain, out_weight):
    tokens_here = qkv.shape[1]
    channels = qkv.shape[2]
    modes = decay_rate.shape[0]
    tail_rows = qkv[:, tokens_here - (KS - 1) :, :]
    previous = passed_along(tail_rows, "seq", 1)
    extended = jnp.concatenate([previous, qkv], axis=1).astype(jnp.float32)
    filtered = jnp.zeros((3, tokens_here, channels), jnp.float32)
    for offset in range(KS):
        start_row = KS - 1 - offset
        filtered = (
            filtered
            + conv_weight[:, offset, None, :] * extended[:, start_row : start_row + tokens_here, :]
        )
    product = filtered[1] * filtered[2]
    group_width = min(channels, 128)
    groups = channels // group_width
    block_len = min(tokens_here, 64)
    block_count = tokens_here // block_len
    x_groups = product.reshape(block_count, block_len, groups, group_width).transpose(2, 0, 1, 3)
    rate_groups = decay_rate.reshape(modes, groups, group_width).transpose(1, 0, 2)
    residue_groups = residue.reshape(modes, groups, group_width).transpose(1, 0, 2)
    inner_part, block_entering, section_state = lax.map(
        partial(inner_block, block_len), (x_groups, rate_groups, residue_groups)
    )
    section_state = section_state.transpose(1, 0, 2).reshape(modes, channels)
    section_decay = jnp.exp(-decay_rate * tokens_here)
    identity = (
        jnp.ones(section_state.shape, jnp.float32),
        jnp.zeros(section_state.shape, jnp.float32),
    )
    prefix = prefix_2((section_decay, section_state), "seq", combine_modes, identity)
    section_entering = prefix[1].reshape(modes, groups, group_width).transpose(1, 0, 2)
    carried = lax.map(
        partial(carry_block, block_len),
        (rate_groups, residue_groups, block_entering, section_entering),
    )
    long_part = (inner_part + carried).transpose(1, 2, 0, 3).reshape(tokens_here, channels)
    long_part = long_part + skip_gain[None, :] * product
    mixed_local = (filtered[0] * long_part).astype(jnp.bfloat16)
    features = lax.all_gather(mixed_local, "tensor", axis=1, tiled=True)
    projected = jnp.dot(
        features,
        lax.all_gather(out_weight, "seq", axis=0, tiled=True),
        preferred_element_type=jnp.float32,
    )
    return projected.astype(jnp.bfloat16)


def solution(mesh):
    return jax.shard_map(
        local,
        mesh=mesh,
        in_specs=(
            P(None, "seq", "tensor"),
            P(None, None, "tensor"),
            P(None, "tensor"),
            P(None, "tensor"),
            P("tensor"),
            P("seq", "tensor"),
        ),
        out_specs=P("seq", "tensor"),
        check_vma=False,
    )
```

profile of v0, /device:TPU:1, one launch (start us, length us, event | category | flops | bytes accessed | tf_op | source)
XLA Modules:
  0.0 445.3 jit_solution(3757608169586370454)
XLA Ops:
  6.5 0.8 slice.31
  7.4 5.4 %collective-permute-start = (bf16[3,2,512]{2,1,0:T(2,128)(2,1)S(1)}, bf16[3,2,512]{2,1,0:T(2,128)(2,1)S(1)}, u32[]{:S(2)}, u32[]{:S(2)}) collective-permute-start(bf16[3,2,512]{2,1,0:T(2,128)(2,1)S(1)} %slice.31), channel_id=1, source_target_pairs={{0,16},{16,32},{32,48},{48,64},{64,80},{80,96},{96,112},{112,128},... | collective-permute-start | bytes 18440 | tf_op jit(solution)/shard_map/ppermute | solution.py:14
  12.7 1.4 multiply_exponential_fusion.2
  14.2 0.9 fusion.35
  15.1 0.9 copy.34
  16.1 0.9 copy.35
  17.4 0.5 fusion.29
  17.9 1.2 copy-done
  19.3 1.1 broadcast.65.clone
  20.4 119.2 %while.50 = (s32[]{:T(128)}, f32[4,4,64,128]{2,1,3,0:T(4,128)}, f32[4,4,16,128]{3,2,1,0:T(8,128)}, f32[4,16,128]{2,1,0:T(8,128)}, f32[4,4,64,128]{3,0,2,1:T(4,12...) while((s32[]{:T(128)}, f32[4,4,64,128]{2,1,3,0:T(4,128)}, ...), condition=%wide.region_3.4_spmd, body=%wide.region_0.3_spmd.sunk | while | flops 32536580 | bytes 16271129 | solution.py:97
  20.5 0.3 multiply_exponential_fusion.6
  20.9 0.5 rev.4
  21.7 1.8 convolution_bitcast_fusion.3
  23.7 0.6 bitcast_dynamic-update-slice_fusion.6
  24.4 0.6 bitcast_dynamic-update-slice_fusion.7
  25.1 0.6 multiply_reduce_fusion.2
  25.9 10.8 %gather_fusion = f32[4096,128]{1,0:T(8,128)S(1)} fusion(f32[64,128]{1,0:T(8,128)S(1)} %bitcast.132, s32[4096]{0:T(1024)S(1)} %broadcast_clamp_fusion.2), kind=kCustom, calls=%fused_computation.clone.1 | custom fusion | bytes 4210688 | tf_op jit(solution)/shard_map/while/body/eval_jaxpr/gather | solution.py:40
  36.7 4.5 %copy.70 = f32[64,64,128]{1,0,2:T(8,128)} copy(f32[64,64,128]{2,1,0:T(8,128)S(1)} %bitcast.133) | data formatting | bytes 4194304 | tf_op jit(solution)/shard_map/while/body/eval_jaxpr/gather | solution.py:40
  41.2 9.0 %fusion.52 = f32[4,4,64,128]{2,1,3,0:T(4,128)} fusion(f32[4,4,64,128]{2,1,3,0:T(4,128)} %get-tuple-element.485, s32[]{:T(128)} %get-tuple-element.484, f32[64,64,128]{1,0,2:T(8,128)} %copy.70, pred[64,64]{1,0:T(8,128)(4,1)S(1)} %subtract_compare_fusion.2, f32[1,4,64,128]{2,1,3,0:T(4,128)S(1)} %copy.71), kind=kOutput, calls=%fused_computation.32.clone.1 | convolution fusion | flops 25690112 | bytes 4592128 | tf_op jit(solution)/shard_map/while/body/eval_jaxpr/tsc,nsc->ntc/dot_general | solution.py:48
  50.7 0.5 rev.4
  51.5 1.8 convolution_bitcast_fusion.3
  53.5 0.6 bitcast_dynamic-update-slice_fusion.6
  54.2 0.6 bitcast_dynamic-update-slice_fusion.7
  54.9 0.6 multiply_reduce_fusion.2
  55.7 10.8 %gather_fusion = f32[4096,128]{1,0:T(8,128)S(1)} fusion(f32[64,128]{1,0:T(8,128)S(1)} %bitcast.132, s32[4096]{0:T(1024)S(1)} %broadcast_clamp_fusion.2), kind=kCustom, calls=%fused_computation.clone.1 | custom fusion | bytes 4210688 | tf_op jit(solution)/shard_map/while/body/eval_jaxpr/gather | solution.py:40
  66.5 4.5 %copy.70 = f32[64,64,128]{1,0,2:T(8,128)} copy(f32[64,64,128]{2,1,0:T(8,128)S(1)} %bitcast.133) | data formatting | bytes 4194304 | tf_op jit(solution)/shard_map/while/body/eval_jaxpr/gather | solution.py:40
  71.0 9.0 %fusion.52 = f32[4,4,64,128]{2,1,3,0:T(4,128)} fusion(f32[4,4,64,128]{2,1,3,0:T(4,128)} %get-tuple-element.485, s32[]{:T(128)} %get-tuple-element.484, f32[64,64,128]{1,0,2:T(8,128)} %copy.70, pred[64,64]{1,0:T(8,128)(4,1)S(1)} %subtract_compare_fusion.2, f32[1,4,64,128]{2,1,3,0:T(4,128)S(1)} %copy.71), kind=kOutput, calls=%fused_computation.32.clone.1 | convolution fusion | flops 25690112 | bytes 4592128 | tf_op jit(solution)/shard_map/while/body/eval_jaxpr/tsc,nsc->ntc/dot_general | solution.py:48
  80.5 0.5 rev.4
  81.3 1.8 convolution_bitcast_fusion.3
  83.4 0.6 bitcast_dynamic-update-slice_fusion.6
  84.0 0.6 bitcast_dynamic-update-slice_fusion.7
  84.7 0.6 multiply_reduce_fusion.2
  85.5 10.8 %gather_fusion = f32[4096,128]{1,0:T(8,128)S(1)} fusion(f32[64,128]{1,0:T(8,128)S(1)} %bitcast.132, s32[4096]{0:T(1024)S(1)} %broadcast_clamp_fusion.2), kind=kCustom, calls=%fused_computation.clone.1 | custom fusion | bytes 4210688 | tf_op jit(solution)/shard_map/while/body/eval_jaxpr/gather | solution.py:40
  96.3 4.5 %copy.70 = f32[64,64,128]{1,0,2:T(8,128)} copy(f32[64,64,128]{2,1,0:T(8,128)S(1)} %bitcast.133) | data formatting | bytes 4194304 | tf_op jit(solution)/shard_map/while/body/eval_jaxpr/gather | solution.py:40
  100.8 9.0 %fusion.52 = f32[4,4,64,128]{2,1,3,0:T(4,128)} fusion(f32[4,4,64,128]{2,1,3,0:T(4,128)} %get-tuple-element.485, s32[]{:T(128)} %get-tuple-element.484, f32[64,64,128]{1,0,2:T(8,128)} %copy.70, pred[64,64]{1,0:T(8,128)(4,1)S(1)} %subtract_compare_fusion.2, f32[1,4,64,128]{2,1,3,0:T(4,128)S(1)} %copy.71), kind=kOutput, calls=%fused_computation.32.clone.1 | convolution fusion | flops 25690112 | bytes 4592128 | tf_op jit(solution)/shard_map/while/body/eval_jaxpr/tsc,nsc->ntc/dot_general | solution.py:48
  110.3 0.5 rev.4
  111.1 1.8 convolution_bitcast_fusion.3
  113.2 0.6 bitcast_dynamic-update-slice_fusion.6
  113.8 0.6 bitcast_dynamic-update-slice_fusion.7
  114.5 0.6 multiply_reduce_fusion.2
  115.3 10.8 %gather_fusion = f32[4096,128]{1,0:T(8,128)S(1)} fusion(f32[64,128]{1,0:T(8,128)S(1)} %bitcast.132, s32[4096]{0:T(1024)S(1)} %broadcast_clamp_fusion.2), kind=kCustom, calls=%fused_computation.clone.1 | custom fusion | bytes 4210688 | tf_op jit(solution)/shard_map/while/body/eval_jaxpr/gather | solution.py:40
  126.1 4.5 %copy.70 = f32[64,64,128]{1,0,2:T(8,128)} copy(f32[64,64,128]{2,1,0:T(8,128)S(1)} %bitcast.133) | data formatting | bytes 4194304 | tf_op jit(solution)/shard_map/while/body/eval_jaxpr/gather | solution.py:40
  130.6 9.0 %fusion.52 = f32[4,4,64,128]{2,1,3,0:T(4,128)} fusion(f32[4,4,64,128]{2,1,3,0:T(4,128)} %get-tuple-element.485, s32[]{:T(128)} %get-tuple-element.484, f32[64,64,128]{1,0,2:T(8,128)} %copy.70, pred[64,64]{1,0:T(8,128)(4,1)S(1)} %subtract_compare_fusion.2, f32[1,4,64,128]{2,1,3,0:T(4,128)S(1)} %copy.71), kind=kOutput, calls=%fused_computation.32.clone.1 | convolution fusion | flops 25690112 | bytes 4592128 | tf_op jit(solution)/shard_map/while/body/eval_jaxpr/tsc,nsc->ntc/dot_general | solution.py:48
  139.6 0.8 copy.39
  140.4 0.6 all_gather_reshape.3
  141.1 70.4 %all-gather.6.cloned.1.call-done = f32[32,16,512]{2,1,0:T(8,128)} async-done(((f32[1,16,512]{2,1,0:T(8,128)}), f32[32,16,512]{2,1,0:T(8,128)}) %all-gather.6.cloned.1.call-update) | async-done | bytes 1048592 | tf_op jit(solution)/shard_map/all_gather | solution.py:19
  211.5 0.8 while.51
  211.5 0.8 bitcast_add_fusion.5
  212.6 11.1 %while.52 = (s32[]{:T(128)}, f32[4,4,64,128]{2,1,3,0:T(4,128)S(1)}, f32[4,4,16,128]{3,2,1,0:T(8,128)}, f32[4,16,128]{1,2,0:T(8,128)S(1)}, f32[4,16,128]{1,2,0:T(...) while((s32[]{:T(128)}, f32[4,4,64,128]{2,1,3,0:T(4,128)S(1)}, f32[4,4,16,128]{3,2,1,0:T(8,128)}, ...), condition=%wide.region_7.8_spmd, body=%wide.region_6.7_spmd.sunk | while | flops 6594566 | bytes 1049197 | solution.py:108
  212.7 0.8 constant_dynamic-slice_fusion.5
  213.7 1.7 fusion.56
  215.5 0.8 constant_dynamic-slice_fusion.5
  216.4 1.7 fusion.56
  218.3 0.8 constant_dynamic-slice_fusion.5
  219.2 1.7 fusion.56
  221.0 0.8 constant_dynamic-slice_fusion.5
  222.0 1.7 fusion.56
  224.0 0.6 reshape.102
  224.8 0.6 copy-done.1
  225.4 0.9 fusion.32
  226.4 0.5 all-gather.10.cloned.1.call-update
  226.9 126.3 %all-gather.8.cloned.1.call-done = bf16[256,8192]{1,0:T(8,128)(2,1)} async-done(((bf16[256,512]{1,0:T(8,128)(2,1)}), bf16[256,8192]{1,0:T(8,128)(2,1)}) %all-gather.8.cloned.1.call-update) | async-done | bytes 4194320 | tf_op jit(solution)/shard_map/all_gather | solution.py:115
  353.2 77.9 %all-gather.10.cloned.1.call-done = bf16[8192,512]{1,0:T(8,128)(2,1)} async-done(((bf16[256,512]{1,0:T(8,128)(2,1)}), bf16[8192,512]{1,0:T(8,128)(2,1)}) %all-gather.10.cloned.1.call-update) | async-done | bytes 8388624 | tf_op jit(solution)/shard_map/all_gather | solution.py:118
  431.1 7.7 %convolution_convert_fusion = bf16[256,512]{1,0:T(8,128)(2,1)} fusion(bf16[256,8192]{1,0:T(8,128)(2,1)} %all-gather.8.cloned.1.call-done, bf16[8192,512]{1,0:T(8,128)(2,1)} %all-gather.10.cloned.1.call-done), kind=kOutput, calls=%fused_computation.53 | convolution fusion | flops 2147614720 | bytes 12845056 | tf_op jit(solution)/shard_map/dot_general | solution.py:116
  (142 shorter events, 7.8 us)
Async XLA Ops:
  6.5 10.6 %copy-start.3 = (bf16[3,256,512]{2,1,0:T(8,128)(2,1)S(1)}, bf16[3,256,512]{2,1,0:T(8,128)(2,1)}, u32[]{:S(2)}) copy-start(bf16[3,256,512]{2,1,0:T(8,128)(2,1)} %param.14) | copy-start | bytes 2359300
  6.5 134.6 %all-gather.12.cloned.1.call-start = ((), (), s32[]{:S(2)}) async-start(), calls=%async_computation.3 | async-start | bytes 1081344 | tf_op jit(solution)/shard_map/all_gather | solution.py:19
  7.4 9.8 %collective-permute-start = (bf16[3,2,512]{2,1,0:T(2,128)(2,1)S(1)}, bf16[3,2,512]{2,1,0:T(2,128)(2,1)S(1)}, u32[]{:S(2)}, u32[]{:S(2)}) collective-permute-start(bf16[3,2,512]{2,1,0:T(2,128)(2,1)S(1)} %slice.31), channel_id=1, source_target_pairs={{0,16},{16,32},{32,48},{48,64},{64,80},{80,96},{96,112},{112,128},... | collective-permute-start | bytes 18440 | tf_op jit(solution)/shard_map/ppermute | solution.py:14
  14.2 197.3 %all-gather.6.cloned.1.call-start = ((), (), s32[]{:S(2)}) async-start(), calls=%async_computation | async-start | bytes 1081344 | tf_op jit(solution)/shard_map/all_gather | solution.py:19
  17.8 1.2 copy-start
  141.0 212.1 %all-gather.8.cloned.1.call-start = ((), (), s32[]{:S(2)}) async-start(), calls=%async_computation.1 | async-start | bytes 4456448 | tf_op jit(solution)/shard_map/all_gather | solution.py:115
  212.6 11.1 %copy-start.2 = (f32[4,4,64,128]{2,1,3,0:T(4,128)S(1)}, f32[4,4,64,128]{2,1,3,0:T(4,128)}, u32[]{:S(2)}) copy-start(f32[4,4,64,128]{2,1,3,0:T(4,128)} %get-tuple-element.148) | copy-start | bytes 1572868
  224.0 1.4 copy-start.1
  224.0 1.4 copy-start.4
  226.3 204.8 %all-gather.10.cloned.1.call-start = ((), (), s32[]{:S(2)}) async-start(), calls=%async_computation.2 | async-start | bytes 8650752 | tf_op jit(solution)/shard_map/all_gather | solution.py:118
Sparse Core Ops, SparseCore 0:
  14.3 70.3 all-gather.11
  141.2 70.2 all-gather.5
  226.5 126.6 all-gather.7
  355.2 75.8 all-gather.9
where the time goes:
time: 448 us; the launch traced here: 445 us
  waiting for transfers between devices  275 us (61%)
  local copies, waits for them, and re-layouts  83.7 us (19%)
  matrix products  57.6 us (13%)
  between operations  13.3 us (3%)
  other arithmetic  9.04 us (2%)
  starting transfers between devices  5.51 us (1%)
    all_gather x1, waiting for transfers between devices, local(): features = lax.all_gather(mixed_local, 'tensor', axis=1, tiled=True)  126 us
    all_gather x1, waiting for transfers between devices, local(): lax.all_gather(out_weight, 'seq', axis=0, tiled=True)  77.9 us
    all_gather x2, waiting for transfers between devices, prefix_2(): gathered = jax.tree.map(lambda a: lax.all_gather(a, axis), part)  70.4 us
    gather x8, local copies, waits for them, and re-layouts, toeplitz(): picked = filter_taps[jnp.maximum(lag_index, 0), :]  61.1 us
    dot_general x4, matrix products, inner_block(): jnp.einsum('tsc,nsc->ntc', toeplitz(filter_taps), x_block, precision=PREC...  36 us
  transfers between devices with their start and end apart: 5, of which 3 were waited for; matrix products, arithmetic and copies ran while one was open for 28% of the time, Pallas kernels for 0%

commit v1 on v0

--- a/solution.py
+++ b/solution.py
@@ -112,7 +112,9 @@
     long_part = (inner_part + carried).transpose(1, 2, 0, 3).reshape(tokens_here, channels)
     long_part = long_part + skip_gain[None, :] * product
     mixed_local = (filtered[0] * long_part).astype(jnp.bfloat16)
-    features = lax.all_gather(mixed_local, "tensor", axis=1, tiled=True)
+    features = jnp.concatenate(
+        lax.all_to_all(jnp.stack([mixed_local] * lax.axis_size("tensor")), "tensor", 0, 0), axis=1
+    )
     projected = jnp.dot(
         features,
         lax.all_gather(out_weight, "seq", axis=0, tiled=True),

time: 448 us -> 365 us (0.81)
  the two profiles are of different devices: /device:TPU:1 before, /device:TPU:451 now
where the time goes in v1:
time: 365 us; the launch traced here: 362 us
  blocking collectives  104 us (28%)
  local copies, waits for them, and re-layouts  85.2 us (23%)
  waiting for transfers between devices  65.7 us (18%)
  matrix products  57.6 us (16%)
  other arithmetic  33 us (9%)
  between operations  13.3 us (4%)
    all_to_all x1, blocking collectives, local(): lax.all_to_all(jnp.stack([mixed_local] * lax.axis_size('tensor')), 'tenso...  104 us
    all_gather x2, waiting for transfers between devices, prefix_2(): gathered = jax.tree.map(lambda a: lax.all_gather(a, axis), part)  65 us
    gather x8, local copies, waits for them, and re-layouts, toeplitz(): picked = filter_taps[jnp.maximum(lag_index, 0), :]  61.2 us
    dot_general x4, matrix products, inner_block(): jnp.einsum('tsc,nsc->ntc', toeplitz(filter_taps), x_block, precision=PREC...  36 us
    add x31, other arithmetic, combine_modes(): return (earlier[0] * later[0], earlier[1] * later[0] + later[1])  24.5 us
    dot_general x1, matrix products, local(): jnp.dot(features, lax.all_gather(out_weight, 'seq', axis=0, tiled=True),...  7.71 us
  transfers between devices with their start and end apart: 4, of which 1 were waited for; matrix products, arithmetic and copies ran while one was open for 46% of the time, Pallas kernels for 0%

profile of v1, /device:TPU:451, one launch (start us, length us, event | category | flops | bytes accessed | tf_op | source)
XLA Modules:
  0.0 362.2 jit_solution(3287141227440573558)
XLA Ops:
  6.5 0.8 slice.31
  7.4 1.3 collective-permute-start
  8.7 1.4 multiply_exponential_fusion.2
  10.1 0.9 fusion.34
  11.0 0.9 copy.35
  12.0 0.9 copy.36
  13.8 1.2 copy-done
  15.2 1.2 broadcast.70.clone
  16.4 119.3 %while.50 = (s32[]{:T(128)}, f32[4,4,64,128]{2,1,3,0:T(4,128)}, f32[4,4,16,128]{3,2,1,0:T(8,128)}, f32[4,16,128]{2,1,0:T(8,128)}, f32[4,4,64,128]{3,0,2,1:T(4,12...) while((s32[]{:T(128)}, f32[4,4,64,128]{2,1,3,0:T(4,128)}, ...), condition=%wide.region_3.4_spmd, body=%wide.region_0.3_spmd.sunk | while | flops 32536580 | bytes 16271129 | solution.py:97
  17.7 1.8 convolution_bitcast_fusion.3
  21.9 10.8 %gather_fusion = f32[4096,128]{1,0:T(8,128)S(1)} fusion(f32[64,128]{1,0:T(8,128)S(1)} %bitcast.125, s32[4096]{0:T(1024)S(1)} %broadcast_clamp_fusion.2), kind=kCustom, calls=%fused_computation.clone.1 | custom fusion | bytes 4210688 | tf_op jit(solution)/shard_map/while/body/eval_jaxpr/gather | solution.py:40
  32.7 4.5 %copy.72 = f32[64,64,128]{1,0,2:T(8,128)} copy(f32[64,64,128]{2,1,0:T(8,128)S(1)} %bitcast.126) | data formatting | bytes 4194304 | tf_op jit(solution)/shard_map/while/body/eval_jaxpr/gather | solution.py:40
  37.2 9.0 %fusion.51 = f32[4,4,64,128]{2,1,3,0:T(4,128)} fusion(f32[4,4,64,128]{2,1,3,0:T(4,128)} %get-tuple-element.485, s32[]{:T(128)} %get-tuple-element.484, f32[64,64,128]{1,0,2:T(8,128)} %copy.72, pred[64,64]{1,0:T(8,128)(4,1)S(1)} %subtract_compare_fusion.2, f32[1,4,64,128]{2,1,3,0:T(4,128)S(1)} %copy.73), kind=kOutput, calls=%fused_computation.32.clone.1 | convolution fusion | flops 25690112 | bytes 4592128 | tf_op jit(solution)/shard_map/while/body/eval_jaxpr/tsc,nsc->ntc/dot_general | solution.py:48
  47.5 1.8 convolution_bitcast_fusion.3
  51.7 10.8 %gather_fusion = f32[4096,128]{1,0:T(8,128)S(1)} fusion(f32[64,128]{1,0:T(8,128)S(1)} %bitcast.125, s32[4096]{0:T(1024)S(1)} %broadcast_clamp_fusion.2), kind=kCustom, calls=%fused_computation.clone.1 | custom fusion | bytes 4210688 | tf_op jit(solution)/shard_map/while/body/eval_jaxpr/gather | solution.py:40
  62.5 4.5 %copy.72 = f32[64,64,128]{1,0,2:T(8,128)} copy(f32[64,64,128]{2,1,0:T(8,128)S(1)} %bitcast.126) | data formatting | bytes 4194304 | tf_op jit(solution)/shard_map/while/body/eval_jaxpr/gather | solution.py:40
  67.0 9.0 %fusion.51 = f32[4,4,64,128]{2,1,3,0:T(4,128)} fusion(f32[4,4,64,128]{2,1,3,0:T(4,128)} %get-tuple-element.485, s32[]{:T(128)} %get-tuple-element.484, f32[64,64,128]{1,0,2:T(8,128)} %copy.72, pred[64,64]{1,0:T(8,128)(4,1)S(1)} %subtract_compare_fusion.2, f32[1,4,64,128]{2,1,3,0:T(4,128)S(1)} %copy.73), kind=kOutput, calls=%fused_computation.32.clone.1 | convolution fusion | flops 25690112 | bytes 4592128 | tf_op jit(solution)/shard_map/while/body/eval_jaxpr/tsc,nsc->ntc/dot_general | solution.py:48
  77.3 1.8 convolution_bitcast_fusion.3
  81.5 10.8 %gather_fusion = f32[4096,128]{1,0:T(8,128)S(1)} fusion(f32[64,128]{1,0:T(8,128)S(1)} %bitcast.125, s32[4096]{0:T(1024)S(1)} %broadcast_clamp_fusion.2), kind=kCustom, calls=%fused_computation.clone.1 | custom fusion | bytes 4210688 | tf_op jit(solution)/shard_map/while/body/eval_jaxpr/gather | solution.py:40
  92.3 4.5 %copy.72 = f32[64,64,128]{1,0,2:T(8,128)} copy(f32[64,64,128]{2,1,0:T(8,128)S(1)} %bitcast.126) | data formatting | bytes 4194304 | tf_op jit(solution)/shard_map/while/body/eval_jaxpr/gather | solution.py:40
  96.9 9.0 %fusion.51 = f32[4,4,64,128]{2,1,3,0:T(4,128)} fusion(f32[4,4,64,128]{2,1,3,0:T(4,128)} %get-tuple-element.485, s32[]{:T(128)} %get-tuple-element.484, f32[64,64,128]{1,0,2:T(8,128)} %copy.72, pred[64,64]{1,0:T(8,128)(4,1)S(1)} %subtract_compare_fusion.2, f32[1,4,64,128]{2,1,3,0:T(4,128)S(1)} %copy.73), kind=kOutput, calls=%fused_computation.32.clone.1 | convolution fusion | flops 25690112 | bytes 4592128 | tf_op jit(solution)/shard_map/while/body/eval_jaxpr/tsc,nsc->ntc/dot_general | solution.py:48
  107.1 1.8 convolution_bitcast_fusion.3
  111.4 10.8 %gather_fusion = f32[4096,128]{1,0:T(8,128)S(1)} fusion(f32[64,128]{1,0:T(8,128)S(1)} %bitcast.125, s32[4096]{0:T(1024)S(1)} %broadcast_clamp_fusion.2), kind=kCustom, calls=%fused_computation.clone.1 | custom fusion | bytes 4210688 | tf_op jit(solution)/shard_map/while/body/eval_jaxpr/gather | solution.py:40
  122.1 4.5 %copy.72 = f32[64,64,128]{1,0,2:T(8,128)} copy(f32[64,64,128]{2,1,0:T(8,128)S(1)} %bitcast.126) | data formatting | bytes 4194304 | tf_op jit(solution)/shard_map/while/body/eval_jaxpr/gather | solution.py:40
  126.7 9.0 %fusion.51 = f32[4,4,64,128]{2,1,3,0:T(4,128)} fusion(f32[4,4,64,128]{2,1,3,0:T(4,128)} %get-tuple-element.485, s32[]{:T(128)} %get-tuple-element.484, f32[64,64,128]{1,0,2:T(8,128)} %copy.72, pred[64,64]{1,0:T(8,128)(4,1)S(1)} %subtract_compare_fusion.2, f32[1,4,64,128]{2,1,3,0:T(4,128)S(1)} %copy.73), kind=kOutput, calls=%fused_computation.32.clone.1 | convolution fusion | flops 25690112 | bytes 4592128 | tf_op jit(solution)/shard_map/while/body/eval_jaxpr/tsc,nsc->ntc/dot_general | solution.py:48
  137.9 65.0 %all-gather.5.cloned.1.call-done = f32[32,16,512]{2,1,0:T(8,128)} async-done(((f32[1,16,512]{2,1,0:T(8,128)}), f32[32,16,512]{2,1,0:T(8,128)}) %all-gather.5.cloned.1.call-update) | async-done | bytes 1048592 | tf_op jit(solution)/shard_map/all_gather | solution.py:19
  202.8 25.3 %while.51 = (s32[]{:T(128)}, f32[16,512]{1,0:T(8,128)S(1)}, s32[]{:T(128)}, f32[32,16,512]{2,1,0:T(8,128)}, f32[32,16,512]{2,1,0:T(8,128)}, /*index=5*/s32[]{:T(128)}, s32[]{:T(128)}, s32[]{:T(128)}) while((s32[]{:T(128)}, f32[16,512]{1,0:T(8,128)S(1)}, s32[]{:T(128)}, f32[32,16,512]{2,1,0:T(8,128)}, f32[32,16,512]{2,1,0:T(8,128)}, ...), condition=%wide.region_5.6_spmd, body=%wide.region_4.5_spmd.sunk | while | flops 16389 | bytes 131195 | solution.py:27
  203.6 0.8 bitcast_add_fusion.5
  204.5 0.8 bitcast_add_fusion.5
  205.3 0.8 bitcast_add_fusion.5
  206.1 0.8 bitcast_add_fusion.5
  206.9 0.8 bitcast_add_fusion.5
  207.7 0.8 bitcast_add_fusion.5
  208.5 0.8 bitcast_add_fusion.5
  209.4 0.8 bitcast_add_fusion.5
  210.2 0.8 bitcast_add_fusion.5
  211.0 0.8 bitcast_add_fusion.5
  211.8 0.8 bitcast_add_fusion.5
  212.6 0.8 bitcast_add_fusion.5
  213.4 0.8 bitcast_add_fusion.5
  214.3 0.8 bitcast_add_fusion.5
  215.1 0.8 bitcast_add_fusion.5
  215.9 0.8 bitcast_add_fusion.5
  216.7 0.8 bitcast_add_fusion.5
  217.5 0.8 bitcast_add_fusion.5
  218.3 0.8 bitcast_add_fusion.5
  219.2 0.8 bitcast_add_fusion.5
  220.0 0.8 bitcast_add_fusion.5
  220.8 0.8 bitcast_add_fusion.5
  221.6 0.8 bitcast_add_fusion.5
  222.4 0.8 bitcast_add_fusion.5
  224.1 0.8 bitcast_add_fusion.5
  224.9 0.8 bitcast_add_fusion.5
  225.7 0.8 bitcast_add_fusion.5
  228.4 11.1 %while.52 = (s32[]{:T(128)}, f32[4,4,64,128]{2,1,3,0:T(4,128)S(1)}, f32[4,4,16,128]{3,2,1,0:T(8,128)}, f32[4,16,128]{1,2,0:T(8,128)S(1)}, f32[4,16,128]{1,2,0:T(...) while((s32[]{:T(128)}, f32[4,4,64,128]{2,1,3,0:T(4,128)S(1)}, f32[4,4,16,128]{3,2,1,0:T(8,128)}, ...), condition=%wide.region_7.8_spmd, body=%wide.region_6.7_spmd.sunk | while | flops 6594566 | bytes 1049197 | solution.py:108
  228.6 0.9 constant_dynamic-slice_fusion.5
  229.6 1.7 fusion.55
  232.3 1.7 fusion.55
  235.1 1.7 fusion.55
  237.9 1.7 fusion.55
  239.6 1.2 add_bitcast_fusion
  240.8 2.0 reshape.117
  243.8 104.1 %all_to_all.5 = bf16[16,256,512]{1,2,0:T(8,128)(2,1)} all-to-all(bf16[16,256,512]{1,2,0:T(8,128)(2,1)S(1)} %stack.5), channel_id=1, replica_groups=mesh['seq'=32,'tensor'=16] {'tensor'}, dimensions={0} | all-to-all | bytes 8388608 | tf_op jit(solution)/shard_map/all_to_all | solution.py:116
  348.0 7.7 %convolution_convert_fusion = bf16[256,512]{1,0:T(8,128)(2,1)} fusion(bf16[256,8192]{0,1:T(8,128)(2,1)} %bitcast.127, bf16[8192,512]{1,0:T(8,128)(2,1)} %all-gather.7.cloned.1.call-done), kind=kOutput, calls=%fused_computation.53 | convolution fusion | flops 2147614720 | bytes 12845056 | tf_op jit(solution)/shard_map/dot_general | solution.py:118
  (172 shorter events, 26.1 us)
Async XLA Ops:
  6.5 6.5 %copy-start.3 = (bf16[3,256,512]{2,1,0:T(8,128)(2,1)S(1)}, bf16[3,256,512]{2,1,0:T(8,128)(2,1)}, u32[]{:S(2)}) copy-start(bf16[3,256,512]{2,1,0:T(8,128)(2,1)} %param.14) | copy-start | bytes 2359300
  6.5 131.3 %all-gather.9.cloned.1.call-start = ((), (), s32[]{:S(2)}) async-start(), calls=%async_computation.3 | async-start | bytes 1081344 | tf_op jit(solution)/shard_map/all_gather | solution.py:19
  7.4 5.6 %collective-permute-start = (bf16[3,2,512]{2,1,0:T(2,128)(2,1)S(1)}, bf16[3,2,512]{2,1,0:T(2,128)(2,1)S(1)}, u32[]{:S(2)}, u32[]{:S(2)}) collective-permute-start(bf16[3,2,512]{2,1,0:T(2,128)(2,1)S(1)} %slice.31), channel_id=1, source_target_pairs={{0,16},{16,32},{32,48},{48,64},{64,80},{80,96},{96,112},{112,128},... | collective-permute-start | bytes 18440 | tf_op jit(solution)/shard_map/ppermute | solution.py:14
  10.1 192.8 %all-gather.5.cloned.1.call-start = ((), (), s32[]{:S(2)}) async-start(), calls=%async_computation.1 | async-start | bytes 1081344 | tf_op jit(solution)/shard_map/all_gather | solution.py:19
  13.7 1.2 copy-start
  137.1 210.8 %all-gather.7.cloned.1.call-start = ((), (), s32[]{:S(2)}) async-start(), calls=%async_computation.2 | async-start | bytes 8650752 | tf_op jit(solution)/shard_map/all_gather | solution.py:120
  228.4 11.1 %copy-start.2 = (f32[4,4,64,128]{2,1,3,0:T(4,128)S(1)}, f32[4,4,64,128]{2,1,3,0:T(4,128)}, u32[]{:S(2)}) copy-start(f32[4,4,64,128]{2,1,3,0:T(4,128)} %get-tuple-element.148) | copy-start | bytes 1572868
  240.8 2.2 copy-start.1
  240.8 2.2 copy-start.4
Sparse Core Ops, SparseCore 0:
  10.2 65.5 all-gather.8
  137.2 65.5 all-gather.4
  205.0 96.8 all-gather.6
